TPU v7x, 32 devices: a whole 2x2x4 slice. The times are simulated.
32 devices in a mesh: row: 8 (over z, core), col: 4 (over y, x).
Axes of the slice: x: 2, y: 2, z: 4, core: 2. Of those that a mesh axis runs over, the one named last changes fastest.
Arguments:
- trunk_in: bfloat16 [1536, 8192], P('col', 'row'), may hold values from -24 to 24
- conv_weight: bfloat16 [5, 1536, 1536], P(None, 'col'), may hold values from -0.0625 to 0.0625
- conv_bias: float32 [1536], P('col'), may hold values from -3 to 3
- norm_gain: float32 [1536], replicated, may hold values from 0.1 to 1.9
- pair_proj: bfloat16 [64, 1536], replicated, may hold values from -0.15625 to 0.15625
- pair_in: bfloat16 [512, 128, 128], P('row', 'col'), may hold values from -6 to 6
- opm_weight: bfloat16 [1024, 128], replicated, may hold values from -0.1875 to 0.1875
- pair_bias: float32 [128], replicated, may hold values from -3 to 3
Outputs:
- trunk_out: bfloat16 [1536, 8192], P('col', 'row')
- pair_out: bfloat16 [512, 128, 128], P('row', 'col')
All inputs are finite; a program needn't handle non-finite values.
Results may differ from a plain program's by a relative error of at most 0.012.
Values may be sent and summed in bfloat16 or wider, within the bound.
No kernel may reach another device: no remote copies, remote signals or barrier semaphores. Data moves between devices by JAX's collectives and lax.ppermute only.
A program may use at most 64 MiB of HBM per device.

v0:
```python
import jax
import jax.numpy as jnp
from jax import lax
from jax.sharding import PartitionSpec as P

TRUNK_CHANNELS = 1536
DILATION_STEP = 8
POOL = 16
OPM = 32
WINDOWS = 4
EPSILON = 1e-05


def with_halo(cells, sides, width):
    for axis, dim in sides:
        count = lax.axis_size(axis)
        ends = count - 1
        head = lax.slice_in_dim(cells, 0, width, axis=dim)
        tail = lax.slice_in_dim(cells, cells.shape[dim] - width, cells.shape[dim], axis=dim)
        cells = jnp.concatenate(
            [
                lax.ppermute(tail, axis, [(i, (i + 1) % count) for i in range(ends)]),
                cells,
                lax.ppermute(head, axis, [((i + 1) % count, i) for i in range(ends)]),
            ],
            axis=dim,
        )
    return cells


def partner_2(block, axis, bit):
    count = lax.axis_size(axis)
    route = []
    for low in range(count):
        high = low | 1 << bit
        if high != low and high < count:
            route += [(low, high), (high, low)]
    return lax.ppermute(block, axis, route)


def per_device(
    trunk_in, conv_weight, conv_bias, norm_gain, pair_proj, pair_in, opm_weight, pair_bias
):
    local_channels = trunk_in.shape[0]
    token_positions = trunk_in.shape[1]
    kernel = conv_weight.shape[0]
    border_width = 2 * DILATION_STEP
    per_window = lax.axis_size("row") // WINDOWS
    row_index = lax.axis_index("row")
    col_index = lax.axis_index("col")
    in_window = row_index % per_window
    source = trunk_in.astype(jnp.float32)
    zero_sum = jnp.zeros((local_channels, token_positions), jnp.float32)
    squares = lax.psum(jnp.sum(source * source, axis=0), "col")
    scale = lax.rsqrt(squares / TRUNK_CHANNELS + EPSILON)[None, :]
    own_gain = lax.dynamic_slice_in_dim(norm_gain, col_index * local_channels, local_channels, 0)
    gelu_output = jax.nn.gelu(source * own_gain[:, None] * scale).astype(jnp.bfloat16)
    padded_trunk = with_halo(gelu_output, (("row", 1),), border_width)
    carried = zero_sum
    piece = lax.all_gather(padded_trunk, "col", axis=0, tiled=True)
    for tap_offset in range(kernel):
        carried = carried + jnp.dot(
            conv_weight[tap_offset],
            piece[:, tap_offset * DILATION_STEP : tap_offset * DILATION_STEP + token_positions],
            preferred_element_type=jnp.float32,
        )
    trunk_out = (source + carried + conv_bias[:, None]).astype(jnp.bfloat16)
    pooled = (
        trunk_out.astype(jnp.float32)
        .reshape(local_channels, token_positions // POOL, POOL)
        .mean(axis=2)
        .astype(jnp.bfloat16)
    )
    own_proj = lax.dynamic_slice_in_dim(pair_proj, col_index * local_channels, local_channels, 1)
    pooled_f = pooled.astype(jnp.float32)
    partial_proj = lax.dot_general(
        pooled, own_proj, (((0,), (1,)), ((), ())), preferred_element_type=jnp.float32
    )
    projected, sums = lax.psum((partial_proj, jnp.sum(pooled_f * pooled_f, axis=0)), "col")
    sides = (projected * lax.rsqrt(sums / TRUNK_CHANNELS + EPSILON)[:, None]).astype(jnp.bfloat16)
    row_side = sides[:, :OPM]
    collected = sides[:, OPM:]
    col_block = pair_in.shape[1]
    pooled_rows = row_side.shape[0]
    for bit_num in range(per_window.bit_length() - 1):
        partner = partner_2(collected, "row", bit_num)
        upper_half = in_window // 2**bit_num % 2 == 1
        collected = jnp.where(
            upper_half,
            jnp.concatenate([partner, collected], axis=0),
            jnp.concatenate([collected, partner], axis=0),
        )
    own_cols = lax.dynamic_slice_in_dim(collected, col_index * col_block, col_block, 0)
    outer = (
        row_side.astype(jnp.float32)[:, None, :, None]
        * own_cols.astype(jnp.float32)[None, :, None, :]
    ).astype(jnp.bfloat16)
    outer = outer.reshape(pooled_rows * col_block, OPM * OPM)
    update = jnp.dot(outer, opm_weight, preferred_element_type=jnp.float32).reshape(pair_in.shape)
    pair_out = (pair_in.astype(jnp.float32) + update + pair_bias).astype(jnp.bfloat16)
    return (trunk_out, pair_out)


def solution(mesh):
    return jax.shard_map(
        per_device,
        mesh=mesh,
        in_specs=(
            P("col", "row"),
            P(None, "col", None),
            P("col"),
            P(),
            P(),
            P("row", "col", None),
            P(),
            P(),
        ),
        out_specs=(P("col", "row"), P("row", "col", None)),
        check_vma=False,
    )
```

profile of v0, /device:TPU:0, one launch (start us, length us, event | category | flops | bytes accessed | tf_op | source)
XLA Modules:
  0.0 115.7 jit_solution(4807338806114271744)
XLA Ops:
  7.2 0.0 copy-start
  7.2 0.0 all-gather.2.cloned.1.call-start
  7.2 1.5 %copy.25 = bf16[384,1024]{0,1:T(8,128)(2,1)S(1)} copy(bf16[384,1024]{1,0:T(8,128)(2,1)} %param.8) | data formatting | bytes 1572864 | tf_op args[0]
  8.8 0.2 fusion.21
  9.0 11.4 %psum.21 = f32[1024]{0:T(1024)S(1)} all-reduce(f32[1024]{0:T(1024)S(1)} %fusion.21), channel_id=1, replica_groups=mesh['row'=8,'col'=4] {'col'}, use_global_device_ids=true, to_apply=%region_1.2 | all-reduce | flops 1024 | bytes 8192 | tf_op jit(solution)/shard_map/psum | solution.py:54
  20.4 0.8 dynamic_slice.9
  21.2 0.7 fusion.16
  21.9 1.3 %collective-permute-start = (bf16[384,16]{0,1:T(8,128)(2,1)S(1)}, bf16[384,16]{0,1:T(8,128)(2,1)S(1)}, u32[]{:S(2)}, u32[]{:S(2)}) collective-permute-start(bf16[384,16]{0,1:T(8,128)(2,1)S(1)} %get-tuple-element.12), channel_id=1, source_target_pairs={{0,4},{4,8},{8,12},{12,16},{16,20},{20,24},{24,28},{1,5},{5,9},{9,... | collective-permute-start | bytes 36872 | tf_op jit(solution)/shard_map/ppermute | solution.py:22
  23.2 1.3 %collective-permute-start.1 = (bf16[384,16]{0,1:T(8,128)(2,1)S(1)}, bf16[384,16]{0,1:T(8,128)(2,1)S(1)}, u32[]{:S(2)}, u32[]{:S(2)}) collective-permute-start(bf16[384,16]{0,1:T(8,128)(2,1)S(1)} %get-tuple-element.13), channel_id=1, source_target_pairs={{4,0},{8,4},{12,8},{16,12},{20,16},{24,20},{28,24},{5,1},{9,5},{13... | collective-permute-start | bytes 36872 | tf_op jit(solution)/shard_map/ppermute | solution.py:24
  24.5 0.0 collective-permute-done
  24.5 3.6 %collective-permute-done.1 = bf16[384,16]{0,1:T(8,128)(2,1)S(1)} collective-permute-done((bf16[384,16]{0,1:T(8,128)(2,1)S(1)}, bf16[384,16]{0,1:T(8,128)(2,1)S(1)}, u32[]{:S(2)}, u32[]{:S(2)}) %collective-permute-start.1) | collective-permute-done | bytes 12320 | tf_op jit(solution)/shard_map/ppermute | solution.py:24
  28.1 1.0 pad_maximum_fusion
  29.1 0.0 all-gather.2.cloned.1.call-update
  29.1 45.1 %all-gather.2.cloned.1.call-done = bf16[1536,1056]{0,1:T(8,128)(2,1)} async-done(((bf16[384,1056]{0,1:T(8,128)(2,1)}), bf16[1536,1056]{0,1:T(8,128)(2,1)}) %all-gather.2.cloned.1.call-update) | async-done | bytes 3244048 | tf_op jit(solution)/shard_map/all_gather | solution.py:60
  74.2 0.0 copy-start.1
  74.2 0.0 slice-start
  74.2 4.2 %fusion.5 = f32[1024,384]{1,0:T(8,128)S(1)} fusion(bf16[1536,1056]{0,1:T(8,128)(2,1)} %all-gather.2.cloned.1.call-done, bf16[5,384,1536]{2,1,0:T(8,128)(2,1)} %param.9), kind=kOutput, calls=%fused_computation.6 | convolution fusion | flops 1207959552 | bytes 5898240 | tf_op jit(solution)/shard_map/dot_general | solution.py:62
  78.4 0.0 copy-done.1
  78.4 0.0 slice-start.1
  78.4 3.2 %fusion.7 = f32[1024,384]{1,0:T(8,128)S(1)} fusion(bf16[1536,1056]{0,1:T(8,128)(2,1)S(1)} %copy-done.1, bf16[5,384,1536]{2,1,0:T(8,128)(2,1)} %param.9), kind=kOutput, calls=%fused_computation.8 | convolution fusion | flops 1207959552 | bytes 5898240 | tf_op jit(solution)/shard_map/dot_general | solution.py:62
  81.6 0.0 slice-done
  81.6 0.0 slice-done.1
  81.6 1.8 %fusion.9 = f32[1024,384]{1,0:T(8,128)S(1)} fusion(bf16[1536,1056]{0,1:T(8,128)(2,1)S(1)} %copy-done.1, bf16[5,384,1536]{2,1,0:T(8,128)(2,1)S(1)} %bitcast.28), kind=kOutput, calls=%fused_computation.10 | convolution fusion | flops 1207959552 | bytes 5898240 | tf_op jit(solution)/shard_map/dot_general | solution.py:62
  83.4 0.0 copy-start.3
  83.5 1.8 %fusion.11 = f32[1024,384]{1,0:T(8,128)S(1)} fusion(bf16[1536,1056]{0,1:T(8,128)(2,1)S(1)} %copy-done.1, bf16[5,384,1536]{2,1,0:T(8,128)(2,1)S(1)} %bitcast.28), kind=kOutput, calls=%fused_computation.12 | convolution fusion | flops 1207959552 | bytes 5898240 | tf_op jit(solution)/shard_map/dot_general | solution.py:62
  85.3 0.0 copy-done.3
  85.3 2.2 %convert_reduce_fusion = (f32[384,64]{0,1:T(8,128)S(1)}, bf16[384,1024]{0,1:T(8,128)(2,1)S(1)}) fusion(f32[384]{0:T(512)S(1)} %copy-done.3, bf16[5,384,1536]{2,1,0:T(8,128)(2,1)S(1)} %bitcast.28, bf16[1536,1056]{0,1:T(8,128)(2,1)S(1)} %copy-done.1, f32[1024,384]{1,0:T(8,128)S(1)} %fusion.5, f32[1024,384]{1,0:T(8,128)S(1)} %fusion.7, ...), kind=kOutput, calls=%fused_computation.30 | convolution fusion | flops 1211867136 | bytes 12290048 | tf_op jit(solution)/shard_map/dot_general | solution.py:62
  87.5 0.1 multiply_reduce_fusion
  87.6 0.9 fusion.41
  88.6 15.8 %all-reduce = (f32[64,64]{0,1:T(8,128)S(1)}, f32[64]{0:T(128)S(1)}) all-reduce(f32[64,64]{0,1:T(8,128)S(1)} %fusion.41, f32[64]{0:T(128)S(1)} %multiply_reduce_fusion), channel_id=1, replica_groups=mesh['row'=8,'col'=4] {'col'}, use_global_device_ids=true, to_apply=%region_3.4 | all-reduce | flops 4160 | bytes 33280 | tf_op jit(solution)/shard_map/psum | solution.py:79
  104.4 0.1 collective-permute-start.2
  104.5 1.2 %copy.29 = bf16[384,1024]{1,0:T(8,128)(2,1)} copy(bf16[384,1024]{0,1:T(8,128)(2,1)S(1)} %get-tuple-element.17) | data formatting | bytes 1572864
  105.7 0.0 copy-start.2
  105.7 0.0 copy-start.4
  105.8 0.2 copy.27
  105.9 0.0 collective-permute-done.2
  106.0 0.1 fusion.44
  106.1 0.1 copy.28
  106.2 0.2 mul.102
  106.4 0.0 copy-done
  106.4 0.3 copy-done.2
  106.8 0.0 copy-done.4
  106.8 2.1 %fusion.29 = bf16[64,32,128]{2,1,0:T(8,128)(2,1)} fusion(f32[32,1024]{1,0:T(8,128)S(1)} %mul.102, f32[64,1024]{1,0:T(8,128)S(1)} %copy.27, bf16[64,32,128]{2,1,0:T(8,128)(2,1)S(1)} %copy-done.2, f32[128]{0:T(128)S(1)} %copy-done.4, bf16[1024,128]{1,0:T(8,128)(2,1)S(1)} %copy-done), kind=kOutput, calls=%fused_computation.33 | convolution fusion | flops 542113792 | bytes 1704448 | tf_op jit(solution)/shard_map/dot_general | solution.py:99
  (8 shorter events, 0.1 us)
Async XLA Ops:
  7.2 99.3 %copy-start = (bf16[1024,128]{1,0:T(8,128)(2,1)S(1)}, bf16[1024,128]{1,0:T(8,128)(2,1)}, u32[]{:S(2)}) copy-start(bf16[1024,128]{1,0:T(8,128)(2,1)} %param.14) | copy-start | bytes 786436
  7.2 67.0 %all-gather.2.cloned.1.call-start = ((), (), s32[]{:S(2)}) async-start(), calls=%async_computation | async-start | bytes 4055040 | tf_op jit(solution)/shard_map/all_gather | solution.py:60
  21.9 2.6 %collective-permute-start = (bf16[384,16]{0,1:T(8,128)(2,1)S(1)}, bf16[384,16]{0,1:T(8,128)(2,1)S(1)}, u32[]{:S(2)}, u32[]{:S(2)}) collective-permute-start(bf16[384,16]{0,1:T(8,128)(2,1)S(1)} %get-tuple-element.12), channel_id=1, source_target_pairs={{0,4},{4,8},{8,12},{12,16},{16,20},{20,24},{24,28},{1,5},{5,9},{9,... | collective-permute-start | bytes 36872 | tf_op jit(solution)/shard_map/ppermute | solution.py:22
  23.2 4.9 %collective-permute-start.1 = (bf16[384,16]{0,1:T(8,128)(2,1)S(1)}, bf16[384,16]{0,1:T(8,128)(2,1)S(1)}, u32[]{:S(2)}, u32[]{:S(2)}) collective-permute-start(bf16[384,16]{0,1:T(8,128)(2,1)S(1)} %get-tuple-element.13), channel_id=1, source_target_pairs={{4,0},{8,4},{12,8},{16,12},{20,16},{24,20},{28,24},{5,1},{9,5},{13... | collective-permute-start | bytes 36872 | tf_op jit(solution)/shard_map/ppermute | solution.py:24
  74.2 4.2 %copy-start.1 = (bf16[1536,1056]{0,1:T(8,128)(2,1)S(1)}, bf16[1536,1056]{0,1:T(8,128)(2,1)}, u32[]{:S(2)}) copy-start(bf16[1536,1056]{0,1:T(8,128)(2,1)} %all-gather.2.cloned.1.call-done) | copy-start | bytes 9732100
  74.2 7.4 %slice-start = ((s8[5898240]{0:T(1024)(128)(4,1)}), s8[4194304]{0:T(1024)(128)(4,1)S(1)}, s32[]{:S(2)}) async-start(s8[5898240]{0:T(1024)(128)(4,1)} %bitcast.27), calls=%async_computation.1 | async-start | bytes 8388608
  78.4 3.2 %slice-start.1 = ((s8[5898240]{0:T(1024)(128)(4,1)}), s8[1703936]{0:T(1024)(128)(4,1)S(1)}, s32[]{:S(2)}) async-start(s8[5898240]{0:T(1024)(128)(4,1)} %bitcast.27), calls=%async_computation.2 | async-start | bytes 3407872
  83.4 1.8 %copy-start.3 = (f32[384]{0:T(512)S(1)}, f32[384]{0:T(512)}, u32[]{:S(2)}) copy-start(f32[384]{0:T(512)} %param.10) | copy-start | bytes 4612
  104.4 1.5 %collective-permute-start.2 = (bf16[64,32]{0,1:T(8,128)(2,1)S(1)}, bf16[64,32]{0,1:T(8,128)(2,1)S(1)}, u32[]{:S(2)}, u32[]{:S(2)}) collective-permute-start(bf16[64,32]{0,1:T(8,128)(2,1)S(1)} %get-tuple-element.15), channel_id=1, source_target_pairs={{0,4},{4,0},{8,12},{12,8},{16,20},{20,16},{24,28},{28,24},{1,5},{5... | collective-permute-start | bytes 12296 | tf_op jit(solution)/shard_map/ppermute | solution.py:38
  105.7 1.0 copy-start.2
  105.7 1.0 copy-start.4
Sparse Core Ops, SparseCore 0:
  29.2 44.9 all-gather.1
where the time goes:
time: 116 us
  waiting for transfers between devices  48.7 us (42%)
  blocking collectives  27.2 us (23%)
  matrix products  16.2 us (14%)
  between operations  14.3 us (12%)
  local copies, waits for them, and re-layouts  4.39 us (4%)
  starting transfers between devices  2.69 us (2%)
  other arithmetic  2.16 us (2%)
    all_gather x1, waiting for transfers between devices, per_device(): piece = lax.all_gather(padded_trunk, 'col', axis=0, tiled=True)  45.1 us
    psum x1, blocking collectives, per_device(): lax.psum((partial_proj, jnp.sum(pooled_f * pooled_f, axis=0)), 'col')  15.8 us
    dot_general x5, matrix products, per_device(): jnp.dot(conv_weight[tap_offset], piece[:, tap_offset * DILATION_STEP:tap_...  13.2 us
    psum x1, blocking collectives, per_device(): squares = lax.psum(jnp.sum(source * source, axis=0), 'col')  11.4 us
    ppermute x1, waiting for transfers between devices, with_halo(): lax.ppermute(head, axis, [((i + 1) % count, i) for i in range(ends)])  3.57 us
    unnamed x16, local copies, waits for them, and re-layouts  3.06 us
  transfers between devices with their start and end apart: 4, of which 2 were waited for; matrix products, arithmetic and copies ran while one was open for 1% of the time, Pallas kernels for 0%

commit v1 on v0

--- a/solution.py
+++ b/solution.py
@@ -57,7 +57,15 @@
     gelu_output = jax.nn.gelu(source * own_gain[:, None] * scale).astype(jnp.bfloat16)
     padded_trunk = with_halo(gelu_output, (("row", 1),), border_width)
     carried = zero_sum
-    piece = lax.all_gather(padded_trunk, "col", axis=0, tiled=True)
+    value_now = lax.axis_size("col")
+    x_new, shaped = (value_now, lax.axis_index("col"))
+    piece, part_now = (padded_trunk, 1)
+    while part_now < x_new:
+        mid_arr = lax.ppermute(piece, "col", [(kk, kk ^ part_now) for kk in range(x_new)])
+        s_next = jnp.concatenate([piece, mid_arr], axis=0)
+        reached = jnp.concatenate([mid_arr, piece], axis=0)
+        piece = jnp.where(shaped & part_now == 0, s_next, reached)
+        part_now = 2 * part_now
     for tap_offset in range(kernel):
         carried = carried + jnp.dot(
             conv_weight[tap_offset],

time: 116 us -> 118 us (1.017)
  between operations: 14.3 us -> 0.91 us
  waiting for transfers between devices: 48.7 us -> 60.7 us
  other arithmetic: 2.16 us -> 8.04 us
  matrix products: 16.2 us -> 13.9 us
    ppermute x0 -> x2, waiting for transfers between devices: none -> 57.1 us  [per_device(): lax.ppermute(piece, 'col', [(kk, kk ^ part_now) for kk in range(x_new)])]
    all_gather x1 -> x0, waiting for transfers between devices: 45.1 us -> none  [per_device(): piece = lax.all_gather(padded_trunk, 'col', axis=0, tiled=True)]
    select_n x0 -> x2, other arithmetic: none -> 6.79 us  [per_device(): piece = jnp.where(shaped & part_now == 0, s_next, reached)]
    dot_general x5, matrix products: 13.2 us -> 10.9 us  [per_device(): jnp.dot(conv_weight[tap_offset], piece[:, tap_offset * DILATION_STEP:tap_...]
    unnamed x16 -> x14, local copies, waits for them, and re-layouts: 3.06 us -> 3.06 us
  transfers between devices with their start and end apart: 4 -> 5, of which waited for: 2 -> 3; matrix products, arithmetic and copies ran while one was open for 1% -> 1% of each run, Pallas kernels for 0% -> 0%
where the time goes in v1:
time: 118 us; the launch traced here: 117 us
  waiting for transfers between devices  60.7 us (51%)
  blocking collectives  26.1 us (22%)
  matrix products  13.9 us (12%)
  other arithmetic  8.04 us (7%)
  local copies, waits for them, and re-layouts  4.4 us (4%)
  starting transfers between devices  3.36 us (3%)
    ppermute x2, waiting for transfers between devices, per_device(): lax.ppermute(piece, 'col', [(kk, kk ^ part_now) for kk in range(x_new)])  57.1 us
    psum x1, blocking collectives, per_device(): lax.psum((partial_proj, jnp.sum(pooled_f * pooled_f, axis=0)), 'col')  14.7 us
    psum x1, blocking collectives, per_device(): squares = lax.psum(jnp.sum(source * source, axis=0), 'col')  11.4 us
    dot_general x5, matrix products, per_device(): jnp.dot(conv_weight[tap_offset], piece[:, tap_offset * DILATION_STEP:tap_...  10.9 us
    select_n x2, other arithmetic, per_device(): piece = jnp.where(shaped & part_now == 0, s_next, reached)  6.79 us
    ppermute x1, waiting for transfers between devices, with_halo(): lax.ppermute(head, axis, [((i + 1) % count, i) for i in range(ends)])  3.57 us
    unnamed x14, local copies, waits for them, and re-layouts  3.06 us
  transfers between devices with their start and end apart: 5, of which 3 were waited for; matrix products, arithmetic and copies ran while one was open for 1% of the time, Pallas kernels for 0%

profile of v1, /device:TPU:0, one launch (start us, length us, event | category | flops | bytes accessed | tf_op | source)
XLA Modules:
  0.0 117.3 jit_solution(9876173266557052427)
XLA Ops:
  0.6 0.0 copy-start
  0.6 1.5 %copy.25 = bf16[384,1024]{0,1:T(8,128)(2,1)S(1)} copy(bf16[384,1024]{1,0:T(8,128)(2,1)} %param.8) | data formatting | bytes 1572864 | tf_op args[0]
  2.2 0.2 fusion.21
  2.4 11.4 %psum.21 = f32[1024]{0:T(1024)S(1)} all-reduce(f32[1024]{0:T(1024)S(1)} %fusion.21), channel_id=1, replica_groups=mesh['row'=8,'col'=4] {'col'}, use_global_device_ids=true, to_apply=%region_1.2 | all-reduce | flops 1024 | bytes 8192 | tf_op jit(solution)/shard_map/psum | solution.py:54
  13.8 0.8 dynamic_slice.9
  14.6 0.7 fusion.16
  15.3 1.3 %collective-permute-start = (bf16[384,16]{0,1:T(8,128)(2,1)S(1)}, bf16[384,16]{0,1:T(8,128)(2,1)S(1)}, u32[]{:S(2)}, u32[]{:S(2)}) collective-permute-start(bf16[384,16]{0,1:T(8,128)(2,1)S(1)} %get-tuple-element.12), channel_id=1, source_target_pairs={{0,4},{4,8},{8,12},{12,16},{16,20},{20,24},{24,28},{1,5},{5,9},{9,... | collective-permute-start | bytes 36872 | tf_op jit(solution)/shard_map/ppermute | solution.py:22
  16.6 1.3 %collective-permute-start.1 = (bf16[384,16]{0,1:T(8,128)(2,1)S(1)}, bf16[384,16]{0,1:T(8,128)(2,1)S(1)}, u32[]{:S(2)}, u32[]{:S(2)}) collective-permute-start(bf16[384,16]{0,1:T(8,128)(2,1)S(1)} %get-tuple-element.13), channel_id=1, source_target_pairs={{4,0},{8,4},{12,8},{16,12},{20,16},{24,20},{28,24},{5,1},{9,5},{13... | collective-permute-start | bytes 36872 | tf_op jit(solution)/shard_map/ppermute | solution.py:24
  17.9 0.0 collective-permute-done
  17.9 3.6 %collective-permute-done.1 = bf16[384,16]{0,1:T(8,128)(2,1)S(1)} collective-permute-done((bf16[384,16]{0,1:T(8,128)(2,1)S(1)}, bf16[384,16]{0,1:T(8,128)(2,1)S(1)}, u32[]{:S(2)}, u32[]{:S(2)}) %collective-permute-start.1) | collective-permute-done | bytes 12320 | tf_op jit(solution)/shard_map/ppermute | solution.py:24
  21.5 0.1 pad_maximum_fusion
  21.6 0.1 collective-permute-start.2
  21.7 19.6 %collective-permute-done.2 = bf16[384,1056]{0,1:T(8,128)(2,1)} collective-permute-done((bf16[384,1056]{0,1:T(8,128)(2,1)S(1)}, bf16[384,1056]{0,1:T(8,128)(2,1)}, u32[]{:S(2)}, u32[]{:S(2)}) %collective-permute-start.2) | collective-permute-done | bytes 811040 | tf_op jit(solution)/shard_map/ppermute | solution.py:64
  41.2 4.1 %maximum_select_fusion.1 = bf16[768,1056]{0,1:T(8,128)(2,1)S(1)} fusion(bf16[384,1056]{0,1:T(8,128)(2,1)} %collective-permute-done.2, bf16[384,16]{0,1:T(8,128)(2,1)S(1)} %collective-permute-done.1, bf16[384,1024]{0,1:T(8,128)(2,1)S(1)} %fusion.16, bf16[384,16]{0,1:T(8,128)(2,1)S(1)} %collective-permute-done, pred[]{:T(512)S(6)} %eq.13), kind=kLoop, calls=%fused_computation.19 | loop fusion | flops 13787136 | bytes 3244033 | tf_op jit(solution)/shard_map/jit(_where)/select_n | solution.py:67
  45.4 0.6 collective-permute-start.3
  46.0 37.5 %collective-permute-done.3 = bf16[768,1056]{0,1:T(8,128)(2,1)} collective-permute-done((bf16[768,1056]{0,1:T(8,128)(2,1)S(1)}, bf16[768,1056]{0,1:T(8,128)(2,1)}, u32[]{:S(2)}, u32[]{:S(2)}) %collective-permute-start.3) | collective-permute-done | bytes 1622048 | tf_op jit(solution)/shard_map/ppermute | solution.py:64
  83.5 0.0 slice-start
  83.5 2.6 %maximum_select_fusion = bf16[1536,1056]{0,1:T(8,128)(2,1)S(1)} fusion(bf16[768,1056]{0,1:T(8,128)(2,1)} %collective-permute-done.3, bf16[768,1056]{0,1:T(8,128)(2,1)S(1)} %maximum_select_fusion.1, pred[]{:T(512)S(6)} %eq.12), kind=kLoop, calls=%fused_computation.4 | loop fusion | flops 14598144 | bytes 6488065 | tf_op jit(solution)/shard_map/jit(_where)/select_n | solution.py:67
  86.2 0.0 slice-start.1
  86.2 3.2 %fusion.5 = f32[1024,384]{1,0:T(8,128)S(1)} fusion(bf16[1536,1056]{0,1:T(8,128)(2,1)S(1)} %maximum_select_fusion, bf16[5,384,1536]{2,1,0:T(8,128)(2,1)} %param.9), kind=kOutput, calls=%fused_computation.7 | convolution fusion | flops 1207959552 | bytes 5898240 | tf_op jit(solution)/shard_map/dot_general | solution.py:70
  89.4 0.0 slice-done
  89.4 0.0 slice-done.1
  89.4 1.8 %fusion.7 = f32[1024,384]{1,0:T(8,128)S(1)} fusion(bf16[1536,1056]{0,1:T(8,128)(2,1)S(1)} %maximum_select_fusion, bf16[5,384,1536]{2,1,0:T(8,128)(2,1)S(1)} %bitcast.30), kind=kOutput, calls=%fused_computation.9 | convolution fusion | flops 1207959552 | bytes 5898240 | tf_op jit(solution)/shard_map/dot_general | solution.py:70
  91.2 1.8 %fusion.9 = f32[1024,384]{1,0:T(8,128)S(1)} fusion(bf16[1536,1056]{0,1:T(8,128)(2,1)S(1)} %maximum_select_fusion, bf16[5,384,1536]{2,1,0:T(8,128)(2,1)S(1)} %bitcast.30), kind=kOutput, calls=%fused_computation.11 | convolution fusion | flops 1207959552 | bytes 5898240 | tf_op jit(solution)/shard_map/dot_general | solution.py:70
  93.1 0.0 copy-start.2
  93.1 1.8 %fusion.11 = f32[1024,384]{1,0:T(8,128)S(1)} fusion(bf16[1536,1056]{0,1:T(8,128)(2,1)S(1)} %maximum_select_fusion, bf16[5,384,1536]{2,1,0:T(8,128)(2,1)S(1)} %bitcast.30), kind=kOutput, calls=%fused_computation.13 | convolution fusion | flops 1207959552 | bytes 5898240 | tf_op jit(solution)/shard_map/dot_general | solution.py:70
  94.9 0.0 copy-done.2
  94.9 2.2 %convert_reduce_fusion = (f32[384,64]{0,1:T(8,128)S(1)}, bf16[384,1024]{0,1:T(8,128)(2,1)S(1)}) fusion(f32[384]{0:T(512)S(1)} %copy-done.2, bf16[5,384,1536]{2,1,0:T(8,128)(2,1)S(1)} %bitcast.30, bf16[1536,1056]{0,1:T(8,128)(2,1)S(1)} %maximum_select_fusion, f32[1024,384]{1,0:T(8,128)S(1)} %fusion.5, f32[1024,384]{1,0:T(8,128)S(1)} %fusion.7, ...), kind=kOutput, calls=%fused_computation.32 | convolution fusion | flops 1211867136 | bytes 12290048 | tf_op jit(solution)/shard_map/dot_general | solution.py:70
  97.1 0.1 multiply_reduce_fusion
  97.2 0.9 fusion.43
  98.2 14.7 %all-reduce = (f32[64,64]{0,1:T(8,128)S(1)}, f32[64]{0:T(128)S(1)}) all-reduce(f32[64,64]{0,1:T(8,128)S(1)} %fusion.43, f32[64]{0:T(128)S(1)} %multiply_reduce_fusion), channel_id=1, replica_groups=mesh['row'=8,'col'=4] {'col'}, use_global_device_ids=true, to_apply=%region_3.4 | all-reduce | flops 4160 | bytes 33280 | tf_op jit(solution)/shard_map/psum | solution.py:87
  112.9 0.1 collective-permute-start.4
  113.0 1.2 copy.29
  114.2 0.0 copy-start.1
  114.2 0.0 copy-start.3
  114.3 0.2 copy.27
  114.4 0.0 collective-permute-done.4
  114.5 0.1 fusion.46
  114.6 0.1 copy.28
  114.7 0.2 mul.102
  114.9 0.0 copy-done
  114.9 0.3 copy-done.1
  115.3 0.0 copy-done.3
  115.3 2.1 %fusion.27 = bf16[64,32,128]{2,1,0:T(8,128)(2,1)} fusion(f32[32,1024]{1,0:T(8,128)S(1)} %mul.102, f32[64,1024]{1,0:T(8,128)S(1)} %copy.27, bf16[64,32,128]{2,1,0:T(8,128)(2,1)S(1)} %copy-done.1, f32[128]{0:T(128)S(1)} %copy-done.3, bf16[1024,128]{1,0:T(8,128)(2,1)S(1)} %copy-done), kind=kOutput, calls=%fused_computation.35 | convolution fusion | flops 542113792 | bytes 1704448 | tf_op jit(solution)/shard_map/dot_general | solution.py:107
  (8 shorter events, 0.1 us)
Async XLA Ops:
  0.6 114.3 %copy-start = (bf16[1024,128]{1,0:T(8,128)(2,1)S(1)}, bf16[1024,128]{1,0:T(8,128)(2,1)}, u32[]{:S(2)}) copy-start(bf16[1024,128]{1,0:T(8,128)(2,1)} %param.14) | copy-start | bytes 786436
  15.3 2.6 %collective-permute-start = (bf16[384,16]{0,1:T(8,128)(2,1)S(1)}, bf16[384,16]{0,1:T(8,128)(2,1)S(1)}, u32[]{:S(2)}, u32[]{:S(2)}) collective-permute-start(bf16[384,16]{0,1:T(8,128)(2,1)S(1)} %get-tuple-element.12), channel_id=1, source_target_pairs={{0,4},{4,8},{8,12},{12,16},{16,20},{20,24},{24,28},{1,5},{5,9},{9,... | collective-permute-start | bytes 36872 | tf_op jit(solution)/shard_map/ppermute | solution.py:22
  16.6 4.9 %collective-permute-start.1 = (bf16[384,16]{0,1:T(8,128)(2,1)S(1)}, bf16[384,16]{0,1:T(8,128)(2,1)S(1)}, u32[]{:S(2)}, u32[]{:S(2)}) collective-permute-start(bf16[384,16]{0,1:T(8,128)(2,1)S(1)} %get-tuple-element.13), channel_id=1, source_target_pairs={{4,0},{8,4},{12,8},{16,12},{20,16},{24,20},{28,24},{5,1},{9,5},{13... | collective-permute-start | bytes 36872 | tf_op jit(solution)/shard_map/ppermute | solution.py:24
  21.6 19.6 %collective-permute-start.2 = (bf16[384,1056]{0,1:T(8,128)(2,1)S(1)}, bf16[384,1056]{0,1:T(8,128)(2,1)}, u32[]{:S(2)}, u32[]{:S(2)}) collective-permute-start(bf16[384,1056]{0,1:T(8,128)(2,1)S(1)} %pad_maximum_fusion), channel_id=1, source_target_pairs={{0,1},{1,0},{2,3},{3,2},{4,5},{5,4},{6,7},{7,6},{8,9},{9,8},{10,11... | collective-permute-start | bytes 2433032 | tf_op jit(solution)/shard_map/ppermute | solution.py:64
  45.4 38.2 %collective-permute-start.3 = (bf16[768,1056]{0,1:T(8,128)(2,1)S(1)}, bf16[768,1056]{0,1:T(8,128)(2,1)}, u32[]{:S(2)}, u32[]{:S(2)}) collective-permute-start(bf16[768,1056]{0,1:T(8,128)(2,1)S(1)} %maximum_select_fusion.1), channel_id=1, source_target_pairs={{0,2},{1,3},{2,0},{3,1},{4,6},{5,7},{6,4},{7,5},{8,10},{9,11},{10,... | collective-permute-start | bytes 4866056 | tf_op jit(solution)/shard_map/ppermute | solution.py:64
  83.5 5.9 %slice-start = ((s8[5898240]{0:T(1024)(128)(4,1)}), s8[4194304]{0:T(1024)(128)(4,1)S(1)}, s32[]{:S(2)}) async-start(s8[5898240]{0:T(1024)(128)(4,1)} %bitcast.29), calls=%async_computation | async-start | bytes 8388608
  86.2 3.2 %slice-start.1 = ((s8[5898240]{0:T(1024)(128)(4,1)}), s8[1703936]{0:T(1024)(128)(4,1)S(1)}, s32[]{:S(2)}) async-start(s8[5898240]{0:T(1024)(128)(4,1)} %bitcast.29), calls=%async_computation.1 | async-start | bytes 3407872
  93.1 1.8 %copy-start.2 = (f32[384]{0:T(512)S(1)}, f32[384]{0:T(512)}, u32[]{:S(2)}) copy-start(f32[384]{0:T(512)} %param.10) | copy-start | bytes 4612
  112.9 1.5 %collective-permute-start.4 = (bf16[64,32]{0,1:T(8,128)(2,1)S(1)}, bf16[64,32]{0,1:T(8,128)(2,1)S(1)}, u32[]{:S(2)}, u32[]{:S(2)}) collective-permute-start(bf16[64,32]{0,1:T(8,128)(2,1)S(1)} %get-tuple-element.15), channel_id=1, source_target_pairs={{0,4},{4,0},{8,12},{12,8},{16,20},{20,16},{24,28},{28,24},{1,5},{5... | collective-permute-start | bytes 12296 | tf_op jit(solution)/shard_map/ppermute | solution.py:38
  114.2 1.0 copy-start.1
  114.2 1.0 copy-start.3
